TPU v7x, 32 devices: a whole 2x2x4 slice. The times are simulated.
32 devices in a mesh: gx: 4 (over z), gy: 4 (over x, core), gz: 2 (over y).
Axes of the slice: x: 2, y: 2, z: 4, core: 2. Of those that a mesh axis runs over, the one named last changes fastest.
Arguments:
- tokens: bfloat16 [64, 128, 3072], P('gx', ('gy', 'gz')), may hold values from -20 to 20
- grads_out: bfloat16 [64, 128, 3072], P('gx', ('gy', 'gz')), may hold values from -6 to 6
- labels: int32 [64, 128, 16], P('gx', ('gy', 'gz')), may hold values from 0 to 2
- ln_gain: float32 [192], replicated, may hold values from 0.1 to 1.9
- qkv_weight: bfloat16 [192, 576], replicated, may hold values from -0.4375 to 0.4375
- proj_weight: bfloat16 [192, 192], replicated, may hold values from -0.4375 to 0.4375
Outputs:
- grad_tokens: bfloat16 [64, 128, 3072], P('gx', ('gy', 'gz'))
- grad_gain: float32 [192], replicated
- grad_qkv: float32 [110592], replicated
- grad_proj: float32 [36864], replicated
Inputs may be any that keep to these rules, and one draw needn't show every extreme that they name: labels are given on the shifted grid.
All inputs are finite; a program needn't handle non-finite values.
Results may differ from a plain program's by a relative error of at most 0.0087.
Values may be sent and summed in bfloat16 or wider, within the bound.
No kernel may reach another device: no remote copies, remote signals or barrier semaphores. Data moves between devices by JAX's collectives and lax.ppermute only.
A program may use at most 64 MiB of HBM per device.

v0:
```python
import jax
import jax.numpy as jnp
from jax import lax
from jax.sharding import PartitionSpec as P

HEADS = 6
C = 192
WIN = 8
SHIFT = 4
NZ = 16


def passed_along(block, axis, distance):
    devices = range(lax.axis_size(axis))
    route = [((i - distance) % len(devices), i) for i in devices]
    return lax.ppermute(block, axis, route)


def to_windows(values):
    extent_a, extent_b, extent_c = (values.shape[0], values.shape[1], values.shape[2])
    trailing = values.shape[3:]
    shaped = values.reshape(
        (extent_a // WIN, WIN, extent_b // WIN, WIN, extent_c // WIN, WIN) + trailing
    )
    axes_order = (0, 2, 4, 1, 3, 5) + tuple(range(6, 6 + len(trailing)))
    return shaped.transpose(axes_order).reshape((-1, WIN**3) + trailing)


def from_windows(values, extent_a, extent_b, extent_c):
    trailing = values.shape[2:]
    shaped = values.reshape(
        (extent_a // WIN, extent_b // WIN, extent_c // WIN, WIN, WIN, WIN) + trailing
    )
    axes_order = (0, 3, 1, 4, 2, 5) + tuple(range(6, 6 + len(trailing)))
    return shaped.transpose(axes_order).reshape((extent_a, extent_b, extent_c) + trailing)


def window_grads(window_tokens, window_grads_out, mask_keys, ln_gain, qkv_weight, proj_weight):
    channels = window_tokens.shape[1]
    head_size = channels // HEADS
    score_scale = head_size ** (-0.5)
    as_float = window_tokens.astype(jnp.float32)
    row_mean = jnp.mean(as_float, axis=1, keepdims=True)
    centred = as_float - row_mean
    inv_std = lax.rsqrt(jnp.mean(centred * centred, axis=1, keepdims=True) + 1e-05)
    x_hat = centred * inv_std
    normed = (x_hat * ln_gain).astype(jnp.bfloat16)
    qkv_rows = jnp.dot(normed, qkv_weight, preferred_element_type=jnp.float32).astype(jnp.bfloat16)
    queries = qkv_rows[:, :channels].reshape(-1, HEADS, head_size)
    keys_all = qkv_rows[:, channels : 2 * channels].reshape(-1, HEADS, head_size)
    values_all = qkv_rows[:, 2 * channels :].reshape(-1, HEADS, head_size)
    scores = (
        jnp.einsum("ihd,jhd->hij", queries, keys_all, preferred_element_type=jnp.float32)
        * score_scale
    )
    allowed = mask_keys[:, None] == mask_keys[None, :]
    weights = jnp.where(allowed[None], jnp.exp(scores), jnp.float32(0.0))
    softmax_probs = weights / jnp.sum(weights, axis=2, keepdims=True)
    probs_bf = softmax_probs.astype(jnp.bfloat16)
    attended = (
        jnp.einsum("hij,jhd->ihd", probs_bf, values_all, preferred_element_type=jnp.float32)
        .reshape(-1, channels)
        .astype(jnp.bfloat16)
    )
    proj_grad = jnp.einsum(
        "tc,td->cd", attended, window_grads_out, preferred_element_type=jnp.float32
    )
    grad_attended = jnp.einsum(
        "tc,dc->td", window_grads_out, proj_weight, preferred_element_type=jnp.float32
    ).astype(jnp.bfloat16)
    grad_heads = grad_attended.reshape(-1, HEADS, head_size)
    grad_probs = jnp.einsum(
        "ihd,jhd->hij", grad_heads, values_all, preferred_element_type=jnp.float32
    )
    grad_values = jnp.einsum(
        "hij,ihd->jhd", probs_bf, grad_heads, preferred_element_type=jnp.float32
    ).astype(jnp.bfloat16)
    row_total = jnp.sum(softmax_probs * grad_probs, axis=2, keepdims=True)
    grad_scores = (softmax_probs * (grad_probs - row_total) * score_scale).astype(jnp.bfloat16)
    grad_queries = jnp.einsum(
        "hij,jhd->ihd", grad_scores, keys_all, preferred_element_type=jnp.float32
    ).astype(jnp.bfloat16)
    grad_keys = jnp.einsum(
        "hij,ihd->jhd", grad_scores, queries, preferred_element_type=jnp.float32
    ).astype(jnp.bfloat16)
    grad_qkv_rows = jnp.concatenate(
        [
            grad_queries.reshape(-1, channels),
            grad_keys.reshape(-1, channels),
            grad_values.reshape(-1, channels),
        ],
        axis=1,
    )
    qkv_grad = jnp.einsum("tc,td->cd", normed, grad_qkv_rows, preferred_element_type=jnp.float32)
    grad_normed = jnp.einsum(
        "td,cd->tc", grad_qkv_rows, qkv_weight, preferred_element_type=jnp.float32
    )
    gain_grad = jnp.sum(grad_normed * x_hat, axis=0)
    scaled_grad = grad_normed * ln_gain
    grad_shifted = inv_std * (
        scaled_grad
        - jnp.mean(scaled_grad, axis=1, keepdims=True)
        - x_hat * jnp.mean(scaled_grad * x_hat, axis=1, keepdims=True)
    )
    return (grad_shifted.astype(jnp.bfloat16), qkv_grad, proj_grad, gain_grad)


def ahead_first(both_arrays):
    arrived = passed_along((both_arrays[0][:SHIFT], both_arrays[1][:SHIFT]), "gx", -1)
    return (
        jnp.concatenate([both_arrays[0][SHIFT:], arrived[0]], axis=0),
        jnp.concatenate([both_arrays[1][SHIFT:], arrived[1]], axis=0),
    )


def ahead_second(both_arrays):
    arrived = passed_along((both_arrays[0][:, :SHIFT], both_arrays[1][:, :SHIFT]), ("gy", "gz"), -1)
    return (
        jnp.concatenate([both_arrays[0][:, SHIFT:], arrived[0]], axis=1),
        jnp.concatenate([both_arrays[1][:, SHIFT:], arrived[1]], axis=1),
    )


def back_first(gradient):
    arrived = passed_along(gradient[-SHIFT:], "gx", 1)
    return jnp.concatenate([arrived, gradient[:-SHIFT]], axis=0)


def back_second(gradient):
    arrived = passed_along(gradient[:, -SHIFT:], ("gy", "gz"), 1)
    return jnp.concatenate([arrived, gradient[:, :-SHIFT]], axis=1)


def per_device(tokens, grads_out, labels, ln_gain, qkv_weight, proj_weight):
    brick_a, brick_b = (tokens.shape[0], tokens.shape[1])
    brick_c = NZ
    channels = C
    both_arrays = (tokens, grads_out)
    both_arrays = ahead_second(ahead_first(both_arrays))
    shifted_tokens = jnp.roll(
        both_arrays[0].reshape(brick_a, brick_b, brick_c, channels), -SHIFT, axis=2
    )
    shifted_grads = jnp.roll(
        both_arrays[1].reshape(brick_a, brick_b, brick_c, channels), -SHIFT, axis=2
    )
    extent_a = brick_a * lax.axis_size("gx")
    extent_b = brick_b * lax.axis_size(("gy", "gz"))
    first_index = lax.axis_index("gx") * brick_a + jnp.arange(brick_a, dtype=jnp.int32)
    second_index = lax.axis_index(("gy", "gz")) * brick_b + jnp.arange(brick_b, dtype=jnp.int32)
    wrap_first = (first_index >= extent_a - SHIFT).astype(jnp.int32)
    wrap_second = (second_index >= extent_b - SHIFT).astype(jnp.int32)
    wrap_third = (jnp.arange(brick_c, dtype=jnp.int32) >= brick_c - SHIFT).astype(jnp.int32)
    region = (
        wrap_first[:, None, None] * 4 + wrap_second[None, :, None] * 2 + wrap_third[None, None, :]
    )
    mask_key = labels * 8 + region

    def window_step(totals, window_item):
        grad_win, qkv_part, proj_part, gain_part = window_grads(
            window_item[0], window_item[1], window_item[2], ln_gain, qkv_weight, proj_weight
        )
        return ((totals[0] + qkv_part, totals[1] + proj_part, totals[2] + gain_part), grad_win)

    zero_sums = (
        jnp.zeros((channels, 3 * channels), jnp.float32),
        jnp.zeros((channels, channels), jnp.float32),
        jnp.zeros((channels,), jnp.float32),
    )
    sums, grad_windows = lax.scan(
        window_step,
        zero_sums,
        (to_windows(shifted_tokens), to_windows(shifted_grads), to_windows(mask_key)),
    )
    qkv_grad, proj_grad, gain_grad = sums
    qkv_grad, proj_grad, gain_grad = lax.psum((qkv_grad, proj_grad, gain_grad), ("gx", "gy", "gz"))
    grad_branch = jnp.roll(from_windows(grad_windows, brick_a, brick_b, brick_c), SHIFT, axis=2)
    grad_branch = grad_branch.reshape(brick_a, brick_b, brick_c * channels)
    grad_branch = back_first(back_second(grad_branch))
    grad_tokens = (grads_out.astype(jnp.float32) + grad_branch.astype(jnp.float32)).astype(
        jnp.bfloat16
    )
    return (grad_tokens, gain_grad, qkv_grad.reshape(-1), proj_grad.reshape(-1))


def solution(mesh):
    return jax.shard_map(
        per_device,
        mesh=mesh,
        in_specs=(
            P("gx", ("gy", "gz"), None),
            P("gx", ("gy", "gz"), None),
            P("gx", ("gy", "gz"), None),
            P(),
            P(),
            P(),
        ),
        out_specs=(P("gx", ("gy", "gz"), None), P(), P(), P()),
        check_vma=False,
    )
```

profile of v0, /device:TPU:0, one launch (start us, length us, event | category | flops | bytes accessed | tf_op | source)
XLA Modules:
  0.0 585.7 jit_solution(5574990165840329090)
XLA Ops:
  9.1 5.0 collective-permute-start.2
  25.8 5.5 collective-permute-done
  60.5 358.1 %while.17 = (s32[]{:T(128)}, f32[192,576]{1,0:T(8,128)}, f32[192,192]{1,0:T(8,128)S(1)}, f32[192]{0:T(256)S(1)}, bf16[8,512,192]{1,2,0:T(8,128)(2,1)}, /*index=5...) while((s32[]{:T(128)}, f32[192,576]{1,0:T(8,128)}, ...), condition=%wide.region_8.9_spmd.clone, body=%wide.region_0.8_spmd.clone.sunk | while | flops 1079349888 | bytes 64495856 | solution.py:169
  70.8 10.9 %fusion.140 = bf16[6,32,512]{2,1,0:T(8,128)(2,1)} fusion(bf16[512,6,32]{0,2,1:T(8,128)(2,1)S(1)} %bitcast.169, f32[6,512,512]{1,2,0:T(8,128)} %fusion.138, f32[6,512,512]{1,2,0:T(8,128)} %get-tuple-element.265, f32[6,512]{1,0:T(8,128)S(1)} %get-tuple-element.266, pred[512,512]{0,1:T(8,128)(4,1)S(1)} %broadcast_compare_fusion.2), kind=kOutput, calls=%fused_computation.15.clone.1 | convolution fusion | flops 118066688 | bytes 13250560 | tf_op jit(solution)/shard_map/while/body/eval_jaxpr/hij,jhd->ihd/dot_general | solution.py:80
  81.7 10.3 %fusion.139 = bf16[6,32,512]{2,1,0:T(8,128)(2,1)S(1)} fusion(bf16[512,6,32]{0,2,1:T(8,128)(2,1)S(1)} %bitcast.167, f32[6,512,512]{1,2,0:T(8,128)} %fusion.138, f32[6,512,512]{1,2,0:T(8,128)} %get-tuple-element.265, f32[6,512]{1,0:T(8,128)S(1)} %get-tuple-element.266, pred[512,512]{0,1:T(8,128)(4,1)S(1)} %broadcast_compare_fusion.2), kind=kOutput, calls=%fused_computation.16.clone.1 | convolution fusion | flops 118066688 | bytes 13250560 | tf_op jit(solution)/shard_map/while/body/eval_jaxpr/hij,ihd->jhd/dot_general | solution.py:83
  97.7 4.4 fusion.141
  114.6 10.9 %fusion.140 = bf16[6,32,512]{2,1,0:T(8,128)(2,1)} fusion(bf16[512,6,32]{0,2,1:T(8,128)(2,1)S(1)} %bitcast.169, f32[6,512,512]{1,2,0:T(8,128)} %fusion.138, f32[6,512,512]{1,2,0:T(8,128)} %get-tuple-element.265, f32[6,512]{1,0:T(8,128)S(1)} %get-tuple-element.266, pred[512,512]{0,1:T(8,128)(4,1)S(1)} %broadcast_compare_fusion.2), kind=kOutput, calls=%fused_computation.15.clone.1 | convolution fusion | flops 118066688 | bytes 13250560 | tf_op jit(solution)/shard_map/while/body/eval_jaxpr/hij,jhd->ihd/dot_general | solution.py:80
  125.5 10.3 %fusion.139 = bf16[6,32,512]{2,1,0:T(8,128)(2,1)S(1)} fusion(bf16[512,6,32]{0,2,1:T(8,128)(2,1)S(1)} %bitcast.167, f32[6,512,512]{1,2,0:T(8,128)} %fusion.138, f32[6,512,512]{1,2,0:T(8,128)} %get-tuple-element.265, f32[6,512]{1,0:T(8,128)S(1)} %get-tuple-element.266, pred[512,512]{0,1:T(8,128)(4,1)S(1)} %broadcast_compare_fusion.2), kind=kOutput, calls=%fused_computation.16.clone.1 | convolution fusion | flops 118066688 | bytes 13250560 | tf_op jit(solution)/shard_map/while/body/eval_jaxpr/hij,ihd->jhd/dot_general | solution.py:83
  159.5 10.9 %fusion.140 = bf16[6,32,512]{2,1,0:T(8,128)(2,1)} fusion(bf16[512,6,32]{0,2,1:T(8,128)(2,1)S(1)} %bitcast.169, f32[6,512,512]{1,2,0:T(8,128)} %fusion.138, f32[6,512,512]{1,2,0:T(8,128)} %get-tuple-element.265, f32[6,512]{1,0:T(8,128)S(1)} %get-tuple-element.266, pred[512,512]{0,1:T(8,128)(4,1)S(1)} %broadcast_compare_fusion.2), kind=kOutput, calls=%fused_computation.15.clone.1 | convolution fusion | flops 118066688 | bytes 13250560 | tf_op jit(solution)/shard_map/while/body/eval_jaxpr/hij,jhd->ihd/dot_general | solution.py:80
  170.4 10.3 %fusion.139 = bf16[6,32,512]{2,1,0:T(8,128)(2,1)S(1)} fusion(bf16[512,6,32]{0,2,1:T(8,128)(2,1)S(1)} %bitcast.167, f32[6,512,512]{1,2,0:T(8,128)} %fusion.138, f32[6,512,512]{1,2,0:T(8,128)} %get-tuple-element.265, f32[6,512]{1,0:T(8,128)S(1)} %get-tuple-element.266, pred[512,512]{0,1:T(8,128)(4,1)S(1)} %broadcast_compare_fusion.2), kind=kOutput, calls=%fused_computation.16.clone.1 | convolution fusion | flops 118066688 | bytes 13250560 | tf_op jit(solution)/shard_map/while/body/eval_jaxpr/hij,ihd->jhd/dot_general | solution.py:83
  204.3 10.9 %fusion.140 = bf16[6,32,512]{2,1,0:T(8,128)(2,1)} fusion(bf16[512,6,32]{0,2,1:T(8,128)(2,1)S(1)} %bitcast.169, f32[6,512,512]{1,2,0:T(8,128)} %fusion.138, f32[6,512,512]{1,2,0:T(8,128)} %get-tuple-element.265, f32[6,512]{1,0:T(8,128)S(1)} %get-tuple-element.266, pred[512,512]{0,1:T(8,128)(4,1)S(1)} %broadcast_compare_fusion.2), kind=kOutput, calls=%fused_computation.15.clone.1 | convolution fusion | flops 118066688 | bytes 13250560 | tf_op jit(solution)/shard_map/while/body/eval_jaxpr/hij,jhd->ihd/dot_general | solution.py:80
  215.2 10.3 %fusion.139 = bf16[6,32,512]{2,1,0:T(8,128)(2,1)S(1)} fusion(bf16[512,6,32]{0,2,1:T(8,128)(2,1)S(1)} %bitcast.167, f32[6,512,512]{1,2,0:T(8,128)} %fusion.138, f32[6,512,512]{1,2,0:T(8,128)} %get-tuple-element.265, f32[6,512]{1,0:T(8,128)S(1)} %get-tuple-element.266, pred[512,512]{0,1:T(8,128)(4,1)S(1)} %broadcast_compare_fusion.2), kind=kOutput, calls=%fused_computation.16.clone.1 | convolution fusion | flops 118066688 | bytes 13250560 | tf_op jit(solution)/shard_map/while/body/eval_jaxpr/hij,ihd->jhd/dot_general | solution.py:83
  249.2 10.9 %fusion.140 = bf16[6,32,512]{2,1,0:T(8,128)(2,1)} fusion(bf16[512,6,32]{0,2,1:T(8,128)(2,1)S(1)} %bitcast.169, f32[6,512,512]{1,2,0:T(8,128)} %fusion.138, f32[6,512,512]{1,2,0:T(8,128)} %get-tuple-element.265, f32[6,512]{1,0:T(8,128)S(1)} %get-tuple-element.266, pred[512,512]{0,1:T(8,128)(4,1)S(1)} %broadcast_compare_fusion.2), kind=kOutput, calls=%fused_computation.15.clone.1 | convolution fusion | flops 118066688 | bytes 13250560 | tf_op jit(solution)/shard_map/while/body/eval_jaxpr/hij,jhd->ihd/dot_general | solution.py:80
  260.1 10.3 %fusion.139 = bf16[6,32,512]{2,1,0:T(8,128)(2,1)S(1)} fusion(bf16[512,6,32]{0,2,1:T(8,128)(2,1)S(1)} %bitcast.167, f32[6,512,512]{1,2,0:T(8,128)} %fusion.138, f32[6,512,512]{1,2,0:T(8,128)} %get-tuple-element.265, f32[6,512]{1,0:T(8,128)S(1)} %get-tuple-element.266, pred[512,512]{0,1:T(8,128)(4,1)S(1)} %broadcast_compare_fusion.2), kind=kOutput, calls=%fused_computation.16.clone.1 | convolution fusion | flops 118066688 | bytes 13250560 | tf_op jit(solution)/shard_map/while/body/eval_jaxpr/hij,ihd->jhd/dot_general | solution.py:83
  294.0 10.9 %fusion.140 = bf16[6,32,512]{2,1,0:T(8,128)(2,1)} fusion(bf16[512,6,32]{0,2,1:T(8,128)(2,1)S(1)} %bitcast.169, f32[6,512,512]{1,2,0:T(8,128)} %fusion.138, f32[6,512,512]{1,2,0:T(8,128)} %get-tuple-element.265, f32[6,512]{1,0:T(8,128)S(1)} %get-tuple-element.266, pred[512,512]{0,1:T(8,128)(4,1)S(1)} %broadcast_compare_fusion.2), kind=kOutput, calls=%fused_computation.15.clone.1 | convolution fusion | flops 118066688 | bytes 13250560 | tf_op jit(solution)/shard_map/while/body/eval_jaxpr/hij,jhd->ihd/dot_general | solution.py:80
  304.9 10.3 %fusion.139 = bf16[6,32,512]{2,1,0:T(8,128)(2,1)S(1)} fusion(bf16[512,6,32]{0,2,1:T(8,128)(2,1)S(1)} %bitcast.167, f32[6,512,512]{1,2,0:T(8,128)} %fusion.138, f32[6,512,512]{1,2,0:T(8,128)} %get-tuple-element.265, f32[6,512]{1,0:T(8,128)S(1)} %get-tuple-element.266, pred[512,512]{0,1:T(8,128)(4,1)S(1)} %broadcast_compare_fusion.2), kind=kOutput, calls=%fused_computation.16.clone.1 | convolution fusion | flops 118066688 | bytes 13250560 | tf_op jit(solution)/shard_map/while/body/eval_jaxpr/hij,ihd->jhd/dot_general | solution.py:83
  338.9 10.9 %fusion.140 = bf16[6,32,512]{2,1,0:T(8,128)(2,1)} fusion(bf16[512,6,32]{0,2,1:T(8,128)(2,1)S(1)} %bitcast.169, f32[6,512,512]{1,2,0:T(8,128)} %fusion.138, f32[6,512,512]{1,2,0:T(8,128)} %get-tuple-element.265, f32[6,512]{1,0:T(8,128)S(1)} %get-tuple-element.266, pred[512,512]{0,1:T(8,128)(4,1)S(1)} %broadcast_compare_fusion.2), kind=kOutput, calls=%fused_computation.15.clone.1 | convolution fusion | flops 118066688 | bytes 13250560 | tf_op jit(solution)/shard_map/while/body/eval_jaxpr/hij,jhd->ihd/dot_general | solution.py:80
  349.8 10.3 %fusion.139 = bf16[6,32,512]{2,1,0:T(8,128)(2,1)S(1)} fusion(bf16[512,6,32]{0,2,1:T(8,128)(2,1)S(1)} %bitcast.167, f32[6,512,512]{1,2,0:T(8,128)} %fusion.138, f32[6,512,512]{1,2,0:T(8,128)} %get-tuple-element.265, f32[6,512]{1,0:T(8,128)S(1)} %get-tuple-element.266, pred[512,512]{0,1:T(8,128)(4,1)S(1)} %broadcast_compare_fusion.2), kind=kOutput, calls=%fused_computation.16.clone.1 | convolution fusion | flops 118066688 | bytes 13250560 | tf_op jit(solution)/shard_map/while/body/eval_jaxpr/hij,ihd->jhd/dot_general | solution.py:83
  383.8 10.9 %fusion.140 = bf16[6,32,512]{2,1,0:T(8,128)(2,1)} fusion(bf16[512,6,32]{0,2,1:T(8,128)(2,1)S(1)} %bitcast.169, f32[6,512,512]{1,2,0:T(8,128)} %fusion.138, f32[6,512,512]{1,2,0:T(8,128)} %get-tuple-element.265, f32[6,512]{1,0:T(8,128)S(1)} %get-tuple-element.266, pred[512,512]{0,1:T(8,128)(4,1)S(1)} %broadcast_compare_fusion.2), kind=kOutput, calls=%fused_computation.15.clone.1 | convolution fusion | flops 118066688 | bytes 13250560 | tf_op jit(solution)/shard_map/while/body/eval_jaxpr/hij,jhd->ihd/dot_general | solution.py:80
  394.7 10.3 %fusion.139 = bf16[6,32,512]{2,1,0:T(8,128)(2,1)S(1)} fusion(bf16[512,6,32]{0,2,1:T(8,128)(2,1)S(1)} %bitcast.167, f32[6,512,512]{1,2,0:T(8,128)} %fusion.138, f32[6,512,512]{1,2,0:T(8,128)} %get-tuple-element.265, f32[6,512]{1,0:T(8,128)S(1)} %get-tuple-element.266, pred[512,512]{0,1:T(8,128)(4,1)S(1)} %broadcast_compare_fusion.2), kind=kOutput, calls=%fused_computation.16.clone.1 | convolution fusion | flops 118066688 | bytes 13250560 | tf_op jit(solution)/shard_map/while/body/eval_jaxpr/hij,ihd->jhd/dot_general | solution.py:83
  428.4 6.9 %collective-permute-start.4 = (bf16[16,4,3072]{2,1,0:T(4,128)(2,1)S(1)}, bf16[16,4,3072]{2,1,0:T(4,128)(2,1)S(1)}, u32[]{:S(2)}, u32[]{:S(2)}) collective-permute-start(bf16[16,4,3072]{2,1,0:T(4,128)(2,1)S(1)} %slice.101), channel_id=1, source_target_pairs={{7,0},{0,1},{1,2},{2,3},{3,4},{4,5},{5,6},{6,7},{15,8},{8,9},{9,10... | collective-permute-start | bytes 1179656 | tf_op jit(solution)/shard_map/ppermute | solution.py:16
  435.3 5.3 collective-permute-done.4
  445.5 41.9 %psum.21 = f32[192]{0:T(256)} all-reduce(f32[192]{0:T(256)S(1)} %get-tuple-element.65), channel_id=1, replica_groups=mesh['gx'=4,'gy'=4,'gz'=2] {'gx','gy','gz'}, use_global_device_ids=true, to_apply=%region_9.10 | all-reduce | flops 192 | bytes 1536 | tf_op jit(solution)/shard_map/psum | solution.py:175
  490.3 85.1 %all-reduce.3.cloned.1.call-done = (f32[110592]{0:T(1024)}, f32[36864]{0:T(1024)}) async-done(((f32[110592]{0:T(1024)}, f32[36864]{0:T(1024)}), (f32[110592]{0:T(1024)}, f32[36864]{0:T(1024)})) %all-reduce.3.cloned.1.call-update) | async-done | bytes 589840 | tf_op jit(solution)/shard_map/psum | solution.py:175
  (280 shorter events, 246.6 us)
Async XLA Ops:
  7.2 9.3 %copy-start.6 = (bf16[16,16,3072]{2,1,0:T(8,128)(2,1)S(1)}, bf16[16,16,3072]{2,1,0:T(8,128)(2,1)}, u32[]{:S(2)}) copy-start(bf16[16,16,3072]{2,1,0:T(8,128)(2,1)} %param.8) | copy-start | bytes 4718596
  7.2 568.3 %all-reduce.3.cloned.1.call-start = ((), (), s32[]{:S(2)}) async-start(), calls=%async_computation | async-start | bytes 1179648 | tf_op jit(solution)/shard_map/psum | solution.py:175
  9.1 14.9 %collective-permute-start.2 = (bf16[4,16,3072]{2,1,0:T(8,128)(2,1)}, bf16[4,16,3072]{2,1,0:T(8,128)(2,1)}, u32[]{:S(2)}, u32[]{:S(2)}) collective-permute-start(bf16[4,16,3072]{2,1,0:T(8,128)(2,1)} %slice.74), channel_id=1, source_target_pairs={{8,0},{16,8},{24,16},{0,24},{9,1},{17,9},{25,17},{1,25},{10,2},{18... | collective-permute-start | bytes 1179656 | tf_op jit(solution)/shard_map/ppermute | solution.py:16
  15.9 15.3 %collective-permute-start = (bf16[4,16,3072]{2,1,0:T(8,128)(2,1)}, bf16[4,16,3072]{2,1,0:T(8,128)(2,1)}, u32[]{:S(2)}, u32[]{:S(2)}) collective-permute-start(bf16[4,16,3072]{2,1,0:T(8,128)(2,1)} %slice.68), channel_id=1, source_target_pairs={{8,0},{16,8},{24,16},{0,24},{9,1},{17,9},{25,17},{1,25},{10,2},{18... | collective-permute-start | bytes 1179656 | tf_op jit(solution)/shard_map/ppermute | solution.py:16
  25.4 10.4 %collective-permute-start.3 = (bf16[16,4,3072]{2,0,1:T(8,128)(2,1)S(1)}, bf16[16,4,3072]{2,0,1:T(8,128)(2,1)S(1)}, u32[]{:S(2)}, u32[]{:S(2)}) collective-permute-start(bf16[16,4,3072]{2,0,1:T(8,128)(2,1)S(1)} %pad_maximum_fusion.10), channel_id=1, source_target_pairs={{1,0},{2,1},{3,2},{4,3},{5,4},{6,5},{7,6},{0,7},{9,8},{10,9},{11,1... | collective-permute-start | bytes 1179656 | tf_op jit(solution)/shard_map/ppermute | solution.py:16
  33.4 10.8 %collective-permute-start.1 = (bf16[16,4,3072]{2,0,1:T(8,128)(2,1)}, bf16[16,4,3072]{2,0,1:T(8,128)(2,1)S(1)}, u32[]{:S(2)}, u32[]{:S(2)}) collective-permute-start(bf16[16,4,3072]{2,0,1:T(8,128)(2,1)} %pad_maximum_fusion.11), channel_id=1, source_target_pairs={{1,0},{2,1},{3,2},{4,3},{5,4},{6,5},{7,6},{0,7},{9,8},{10,9},{11,1... | collective-permute-start | bytes 1179656 | tf_op jit(solution)/shard_map/ppermute | solution.py:16
  92.0 4.4 copy-start.10
  97.7 5.6 copy-start.12
  135.8 4.4 copy-start.10
  141.6 5.6 copy-start.12
  180.7 4.4 copy-start.10
  186.4 5.6 copy-start.12
  225.5 4.4 copy-start.10
  231.3 5.6 copy-start.12
  270.4 4.4 copy-start.10
  276.1 5.6 copy-start.12
  315.2 4.4 copy-start.10
  321.0 5.6 copy-start.12
  360.1 4.4 copy-start.10
  365.9 5.6 copy-start.12
  410.7 5.6 copy-start.12
  428.1 59.3 %copy-start.1 = (bf16[16,16,3072]{2,1,0:T(8,128)(2,1)S(1)}, bf16[16,16,3072]{2,1,0:T(8,128)(2,1)}, u32[]{:S(2)}) copy-start(bf16[16,16,3072]{2,1,0:T(8,128)(2,1)} %param.9) | copy-start | bytes 4718596
  428.4 12.2 %collective-permute-start.4 = (bf16[16,4,3072]{2,1,0:T(4,128)(2,1)S(1)}, bf16[16,4,3072]{2,1,0:T(4,128)(2,1)S(1)}, u32[]{:S(2)}, u32[]{:S(2)}) collective-permute-start(bf16[16,4,3072]{2,1,0:T(4,128)(2,1)S(1)} %slice.101), channel_id=1, source_target_pairs={{7,0},{0,1},{1,2},{2,3},{3,4},{4,5},{5,6},{6,7},{15,8},{8,9},{9,10... | collective-permute-start | bytes 1179656 | tf_op jit(solution)/shard_map/ppermute | solution.py:16
  442.2 45.2 %collective-permute-start.5 = (bf16[4,16,3072]{2,1,0:T(8,128)(2,1)}, bf16[4,16,3072]{2,1,0:T(8,128)(2,1)}, u32[]{:S(2)}, u32[]{:S(2)}) collective-permute-start(bf16[4,16,3072]{2,1,0:T(8,128)(2,1)} %pad_maximum_fusion.9), channel_id=1, source_target_pairs={{24,0},{0,8},{8,16},{16,24},{25,1},{1,9},{9,17},{17,25},{26,2},{2,... | collective-permute-start | bytes 1179656 | tf_op jit(solution)/shard_map/ppermute | solution.py:16
  (18 other events, 33.1 us)
Sparse Core Ops, SparseCore 0:
  445.6 129.8 all-reduce.2
where the time goes:
time: 587 us; the launch traced here: 586 us
  matrix products  347 us (59%)
  waiting for transfers between devices  99.7 us (17%)
  local copies, waits for them, and re-layouts  46.5 us (8%)
  blocking collectives  41.9 us (7%)
  other arithmetic  21.2 us (4%)
  between operations  14.3 us (2%)
  starting transfers between devices  14 us (2%)
    dot_general x8, matrix products, window_grads(): jnp.einsum('hij,jhd->ihd', grad_scores, keys_all, preferred_element_type=...  87.2 us
    psum x1, waiting for transfers between devices, per_device(): lax.psum((qkv_grad, proj_grad, gain_grad), ('gx', 'gy', 'gz'))  85.1 us
    dot_general x8, matrix products, window_grads(): jnp.einsum('hij,ihd->jhd', grad_scores, queries, preferred_element_type=j...  82.4 us
    psum x1, blocking collectives, per_device(): lax.psum((qkv_grad, proj_grad, gain_grad), ('gx', 'gy', 'gz'))  41.9 us
    dot_general x8, matrix products, window_grads(): jnp.einsum('hij,jhd->ihd', probs_bf, values_all, preferred_element_type=j...  35.3 us
    dot_general x8, matrix products, window_grads(): jnp.einsum('hij,ihd->jhd', probs_bf, grad_heads, preferred_element_type=j...  35.3 us
    dot_general x8, matrix products, window_grads(): jnp.einsum('ihd,jhd->hij', queries, keys_all, preferred_element_type=jnp....  34.3 us
    dot_general x8, matrix products, window_grads(): jnp.einsum('ihd,jhd->hij', grad_heads, values_all, preferred_element_type...  29.5 us
  transfers between devices with their start and end apart: 7, of which 4 were waited for; matrix products, arithmetic and copies ran while one was open for 4% of the time, Pallas kernels for 0%

commit v1 on v0

--- a/solution.py
+++ b/solution.py
@@ -172,7 +172,9 @@
         (to_windows(shifted_tokens), to_windows(shifted_grads), to_windows(mask_key)),
     )
     qkv_grad, proj_grad, gain_grad = sums
-    qkv_grad, proj_grad, gain_grad = lax.psum((qkv_grad, proj_grad, gain_grad), ("gx", "gy", "gz"))
+    qkv_grad, proj_grad, gain_grad = lax.psum(
+        lax.psum((qkv_grad, proj_grad, gain_grad), ("gy", "gz")), "gx"
+    )
     grad_branch = jnp.roll(from_windows(grad_windows, brick_a, brick_b, brick_c), SHIFT, axis=2)
     grad_branch = grad_branch.reshape(brick_a, brick_b, brick_c * channels)
     grad_branch = back_first(back_second(grad_branch))

time: 587 us -> 554 us (0.944)
  waiting for transfers between devices: 99.7 us -> 81.3 us
  blocking collectives: 41.9 us -> 27.2 us
    psum x1 -> x2, waiting for transfers between devices: 85.1 us -> 66.7 us  [the longest x1 36.2 us: per_device(): lax.psum(lax.psum((qkv_grad, proj_grad, gain_grad), ('gy', 'gz')), 'gx')]
    psum x1 -> x2, blocking collectives: 41.9 us -> 27.2 us  [the longest x1 14.8 us: per_device(): lax.psum((qkv_grad, proj_grad, gain_grad), ('gy', 'gz'))]
  transfers between devices with their start and end apart: 7 -> 8, of which waited for: 4 -> 5; matrix products, arithmetic and copies ran while one was open for 4% -> 5% of each run, Pallas kernels for 0% -> 0%
where the time goes in v1:
time: 554 us; the launch traced here: 552 us
  matrix products  347 us (63%)
  waiting for transfers between devices  81.3 us (15%)
  local copies, waits for them, and re-layouts  46.7 us (8%)
  blocking collectives  27.2 us (5%)
  other arithmetic  21.1 us (4%)
  between operations  14.3 us (3%)
  starting transfers between devices  14 us (3%)
    dot_general x8, matrix products, window_grads(): jnp.einsum('hij,jhd->ihd', grad_scores, keys_all, preferred_element_type=...  87.1 us
    dot_general x8, matrix products, window_grads(): jnp.einsum('hij,ihd->jhd', grad_scores, queries, preferred_element_type=j...  82.4 us
    psum x1, waiting for transfers between devices, per_device(): lax.psum(lax.psum((qkv_grad, proj_grad, gain_grad), ('gy', 'gz')), 'gx')  36.2 us
    dot_general x8, matrix products, window_grads(): jnp.einsum('hij,jhd->ihd', probs_bf, values_all, preferred_element_type=j...  35.3 us
    dot_general x8, matrix products, window_grads(): jnp.einsum('hij,ihd->jhd', probs_bf, grad_heads, preferred_element_type=j...  35.3 us
    dot_general x8, matrix products, window_grads(): jnp.einsum('ihd,jhd->hij', queries, keys_all, preferred_element_type=jnp....  34.4 us
    psum x1, waiting for transfers between devices, per_device(): lax.psum((qkv_grad, proj_grad, gain_grad), ('gy', 'gz'))  30.4 us
    dot_general x8, matrix products, window_grads(): jnp.einsum('ihd,jhd->hij', grad_heads, values_all, preferred_element_type...  29.5 us
  transfers between devices with their start and end apart: 8, of which 5 were waited for; matrix products, arithmetic and copies ran while one was open for 5% of the time, Pallas kernels for 0%

profile of v1, /device:TPU:0, one launch (start us, length us, event | category | flops | bytes accessed | tf_op | source)
XLA Modules:
  0.0 552.5 jit_solution(17655053516040953862)
XLA Ops:
  25.8 5.5 collective-permute-done
  60.5 357.9 %while.17 = (s32[]{:T(128)}, f32[192,576]{1,0:T(8,128)}, f32[192,192]{1,0:T(8,128)S(1)}, f32[192]{0:T(256)S(1)}, bf16[8,512,192]{1,2,0:T(8,128)(2,1)}, /*index=5...) while((s32[]{:T(128)}, f32[192,576]{1,0:T(8,128)}, ...), condition=%wide.region_8.9_spmd.clone, body=%wide.region_0.8_spmd.clone.sunk | while | flops 1079349888 | bytes 64495856 | solution.py:169
  70.7 10.9 %fusion.140 = bf16[6,32,512]{2,1,0:T(8,128)(2,1)} fusion(bf16[512,6,32]{0,2,1:T(8,128)(2,1)S(1)} %bitcast.169, f32[6,512,512]{1,2,0:T(8,128)} %fusion.138, f32[6,512,512]{1,2,0:T(8,128)} %get-tuple-element.267, f32[6,512]{1,0:T(8,128)S(1)} %get-tuple-element.268, pred[512,512]{0,1:T(8,128)(4,1)S(1)} %broadcast_compare_fusion.2), kind=kOutput, calls=%fused_computation.15.clone.1 | convolution fusion | flops 118066688 | bytes 13250560 | tf_op jit(solution)/shard_map/while/body/eval_jaxpr/hij,jhd->ihd/dot_general | solution.py:80
  81.6 10.3 %fusion.139 = bf16[6,32,512]{2,1,0:T(8,128)(2,1)S(1)} fusion(bf16[512,6,32]{0,2,1:T(8,128)(2,1)S(1)} %bitcast.167, f32[6,512,512]{1,2,0:T(8,128)} %fusion.138, f32[6,512,512]{1,2,0:T(8,128)} %get-tuple-element.267, f32[6,512]{1,0:T(8,128)S(1)} %get-tuple-element.268, pred[512,512]{0,1:T(8,128)(4,1)S(1)} %broadcast_compare_fusion.2), kind=kOutput, calls=%fused_computation.16.clone.1 | convolution fusion | flops 118066688 | bytes 13250560 | tf_op jit(solution)/shard_map/while/body/eval_jaxpr/hij,ihd->jhd/dot_general | solution.py:83
  114.5 10.9 %fusion.140 = bf16[6,32,512]{2,1,0:T(8,128)(2,1)} fusion(bf16[512,6,32]{0,2,1:T(8,128)(2,1)S(1)} %bitcast.169, f32[6,512,512]{1,2,0:T(8,128)} %fusion.138, f32[6,512,512]{1,2,0:T(8,128)} %get-tuple-element.267, f32[6,512]{1,0:T(8,128)S(1)} %get-tuple-element.268, pred[512,512]{0,1:T(8,128)(4,1)S(1)} %broadcast_compare_fusion.2), kind=kOutput, calls=%fused_computation.15.clone.1 | convolution fusion | flops 118066688 | bytes 13250560 | tf_op jit(solution)/shard_map/while/body/eval_jaxpr/hij,jhd->ihd/dot_general | solution.py:80
  125.4 10.3 %fusion.139 = bf16[6,32,512]{2,1,0:T(8,128)(2,1)S(1)} fusion(bf16[512,6,32]{0,2,1:T(8,128)(2,1)S(1)} %bitcast.167, f32[6,512,512]{1,2,0:T(8,128)} %fusion.138, f32[6,512,512]{1,2,0:T(8,128)} %get-tuple-element.267, f32[6,512]{1,0:T(8,128)S(1)} %get-tuple-element.268, pred[512,512]{0,1:T(8,128)(4,1)S(1)} %broadcast_compare_fusion.2), kind=kOutput, calls=%fused_computation.16.clone.1 | convolution fusion | flops 118066688 | bytes 13250560 | tf_op jit(solution)/shard_map/while/body/eval_jaxpr/hij,ihd->jhd/dot_general | solution.py:83
  159.4 10.9 %fusion.140 = bf16[6,32,512]{2,1,0:T(8,128)(2,1)} fusion(bf16[512,6,32]{0,2,1:T(8,128)(2,1)S(1)} %bitcast.169, f32[6,512,512]{1,2,0:T(8,128)} %fusion.138, f32[6,512,512]{1,2,0:T(8,128)} %get-tuple-element.267, f32[6,512]{1,0:T(8,128)S(1)} %get-tuple-element.268, pred[512,512]{0,1:T(8,128)(4,1)S(1)} %broadcast_compare_fusion.2), kind=kOutput, calls=%fused_computation.15.clone.1 | convolution fusion | flops 118066688 | bytes 13250560 | tf_op jit(solution)/shard_map/while/body/eval_jaxpr/hij,jhd->ihd/dot_general | solution.py:80
  170.3 10.3 %fusion.139 = bf16[6,32,512]{2,1,0:T(8,128)(2,1)S(1)} fusion(bf16[512,6,32]{0,2,1:T(8,128)(2,1)S(1)} %bitcast.167, f32[6,512,512]{1,2,0:T(8,128)} %fusion.138, f32[6,512,512]{1,2,0:T(8,128)} %get-tuple-element.267, f32[6,512]{1,0:T(8,128)S(1)} %get-tuple-element.268, pred[512,512]{0,1:T(8,128)(4,1)S(1)} %broadcast_compare_fusion.2), kind=kOutput, calls=%fused_computation.16.clone.1 | convolution fusion | flops 118066688 | bytes 13250560 | tf_op jit(solution)/shard_map/while/body/eval_jaxpr/hij,ihd->jhd/dot_general | solution.py:83
  204.2 10.9 %fusion.140 = bf16[6,32,512]{2,1,0:T(8,128)(2,1)} fusion(bf16[512,6,32]{0,2,1:T(8,128)(2,1)S(1)} %bitcast.169, f32[6,512,512]{1,2,0:T(8,128)} %fusion.138, f32[6,512,512]{1,2,0:T(8,128)} %get-tuple-element.267, f32[6,512]{1,0:T(8,128)S(1)} %get-tuple-element.268, pred[512,512]{0,1:T(8,128)(4,1)S(1)} %broadcast_compare_fusion.2), kind=kOutput, calls=%fused_computation.15.clone.1 | convolution fusion | flops 118066688 | bytes 13250560 | tf_op jit(solution)/shard_map/while/body/eval_jaxpr/hij,jhd->ihd/dot_general | solution.py:80
  215.1 10.3 %fusion.139 = bf16[6,32,512]{2,1,0:T(8,128)(2,1)S(1)} fusion(bf16[512,6,32]{0,2,1:T(8,128)(2,1)S(1)} %bitcast.167, f32[6,512,512]{1,2,0:T(8,128)} %fusion.138, f32[6,512,512]{1,2,0:T(8,128)} %get-tuple-element.267, f32[6,512]{1,0:T(8,128)S(1)} %get-tuple-element.268, pred[512,512]{0,1:T(8,128)(4,1)S(1)} %broadcast_compare_fusion.2), kind=kOutput, calls=%fused_computation.16.clone.1 | convolution fusion | flops 118066688 | bytes 13250560 | tf_op jit(solution)/shard_map/while/body/eval_jaxpr/hij,ihd->jhd/dot_general | solution.py:83
  249.0 10.9 %fusion.140 = bf16[6,32,512]{2,1,0:T(8,128)(2,1)} fusion(bf16[512,6,32]{0,2,1:T(8,128)(2,1)S(1)} %bitcast.169, f32[6,512,512]{1,2,0:T(8,128)} %fusion.138, f32[6,512,512]{1,2,0:T(8,128)} %get-tuple-element.267, f32[6,512]{1,0:T(8,128)S(1)} %get-tuple-element.268, pred[512,512]{0,1:T(8,128)(4,1)S(1)} %broadcast_compare_fusion.2), kind=kOutput, calls=%fused_computation.15.clone.1 | convolution fusion | flops 118066688 | bytes 13250560 | tf_op jit(solution)/shard_map/while/body/eval_jaxpr/hij,jhd->ihd/dot_general | solution.py:80
  259.9 10.3 %fusion.139 = bf16[6,32,512]{2,1,0:T(8,128)(2,1)S(1)} fusion(bf16[512,6,32]{0,2,1:T(8,128)(2,1)S(1)} %bitcast.167, f32[6,512,512]{1,2,0:T(8,128)} %fusion.138, f32[6,512,512]{1,2,0:T(8,128)} %get-tuple-element.267, f32[6,512]{1,0:T(8,128)S(1)} %get-tuple-element.268, pred[512,512]{0,1:T(8,128)(4,1)S(1)} %broadcast_compare_fusion.2), kind=kOutput, calls=%fused_computation.16.clone.1 | convolution fusion | flops 118066688 | bytes 13250560 | tf_op jit(solution)/shard_map/while/body/eval_jaxpr/hij,ihd->jhd/dot_general | solution.py:83
  293.9 10.9 %fusion.140 = bf16[6,32,512]{2,1,0:T(8,128)(2,1)} fusion(bf16[512,6,32]{0,2,1:T(8,128)(2,1)S(1)} %bitcast.169, f32[6,512,512]{1,2,0:T(8,128)} %fusion.138, f32[6,512,512]{1,2,0:T(8,128)} %get-tuple-element.267, f32[6,512]{1,0:T(8,128)S(1)} %get-tuple-element.268, pred[512,512]{0,1:T(8,128)(4,1)S(1)} %broadcast_compare_fusion.2), kind=kOutput, calls=%fused_computation.15.clone.1 | convolution fusion | flops 118066688 | bytes 13250560 | tf_op jit(solution)/shard_map/while/body/eval_jaxpr/hij,jhd->ihd/dot_general | solution.py:80
  304.8 10.3 %fusion.139 = bf16[6,32,512]{2,1,0:T(8,128)(2,1)S(1)} fusion(bf16[512,6,32]{0,2,1:T(8,128)(2,1)S(1)} %bitcast.167, f32[6,512,512]{1,2,0:T(8,128)} %fusion.138, f32[6,512,512]{1,2,0:T(8,128)} %get-tuple-element.267, f32[6,512]{1,0:T(8,128)S(1)} %get-tuple-element.268, pred[512,512]{0,1:T(8,128)(4,1)S(1)} %broadcast_compare_fusion.2), kind=kOutput, calls=%fused_computation.16.clone.1 | convolution fusion | flops 118066688 | bytes 13250560 | tf_op jit(solution)/shard_map/while/body/eval_jaxpr/hij,ihd->jhd/dot_general | solution.py:83
  338.7 10.9 %fusion.140 = bf16[6,32,512]{2,1,0:T(8,128)(2,1)} fusion(bf16[512,6,32]{0,2,1:T(8,128)(2,1)S(1)} %bitcast.169, f32[6,512,512]{1,2,0:T(8,128)} %fusion.138, f32[6,512,512]{1,2,0:T(8,128)} %get-tuple-element.267, f32[6,512]{1,0:T(8,128)S(1)} %get-tuple-element.268, pred[512,512]{0,1:T(8,128)(4,1)S(1)} %broadcast_compare_fusion.2), kind=kOutput, calls=%fused_computation.15.clone.1 | convolution fusion | flops 118066688 | bytes 13250560 | tf_op jit(solution)/shard_map/while/body/eval_jaxpr/hij,jhd->ihd/dot_general | solution.py:80
  349.6 10.3 %fusion.139 = bf16[6,32,512]{2,1,0:T(8,128)(2,1)S(1)} fusion(bf16[512,6,32]{0,2,1:T(8,128)(2,1)S(1)} %bitcast.167, f32[6,512,512]{1,2,0:T(8,128)} %fusion.138, f32[6,512,512]{1,2,0:T(8,128)} %get-tuple-element.267, f32[6,512]{1,0:T(8,128)S(1)} %get-tuple-element.268, pred[512,512]{0,1:T(8,128)(4,1)S(1)} %broadcast_compare_fusion.2), kind=kOutput, calls=%fused_computation.16.clone.1 | convolution fusion | flops 118066688 | bytes 13250560 | tf_op jit(solution)/shard_map/while/body/eval_jaxpr/hij,ihd->jhd/dot_general | solution.py:83
  383.5 10.9 %fusion.140 = bf16[6,32,512]{2,1,0:T(8,128)(2,1)} fusion(bf16[512,6,32]{0,2,1:T(8,128)(2,1)S(1)} %bitcast.169, f32[6,512,512]{1,2,0:T(8,128)} %fusion.138, f32[6,512,512]{1,2,0:T(8,128)} %get-tuple-element.267, f32[6,512]{1,0:T(8,128)S(1)} %get-tuple-element.268, pred[512,512]{0,1:T(8,128)(4,1)S(1)} %broadcast_compare_fusion.2), kind=kOutput, calls=%fused_computation.15.clone.1 | convolution fusion | flops 118066688 | bytes 13250560 | tf_op jit(solution)/shard_map/while/body/eval_jaxpr/hij,jhd->ihd/dot_general | solution.py:80
  394.4 10.3 %fusion.139 = bf16[6,32,512]{2,1,0:T(8,128)(2,1)S(1)} fusion(bf16[512,6,32]{0,2,1:T(8,128)(2,1)S(1)} %bitcast.167, f32[6,512,512]{1,2,0:T(8,128)} %fusion.138, f32[6,512,512]{1,2,0:T(8,128)} %get-tuple-element.267, f32[6,512]{1,0:T(8,128)S(1)} %get-tuple-element.268, pred[512,512]{0,1:T(8,128)(4,1)S(1)} %broadcast_compare_fusion.2), kind=kOutput, calls=%fused_computation.16.clone.1 | convolution fusion | flops 118066688 | bytes 13250560 | tf_op jit(solution)/shard_map/while/body/eval_jaxpr/hij,ihd->jhd/dot_general | solution.py:83
  428.2 6.9 %collective-permute-start.4 = (bf16[16,4,3072]{2,1,0:T(4,128)(2,1)S(1)}, bf16[16,4,3072]{2,1,0:T(4,128)(2,1)S(1)}, u32[]{:S(2)}, u32[]{:S(2)}) collective-permute-start(bf16[16,4,3072]{2,1,0:T(4,128)(2,1)S(1)} %slice.101), channel_id=1, source_target_pairs={{7,0},{0,1},{1,2},{2,3},{3,4},{4,5},{5,6},{6,7},{15,8},{8,9},{9,10... | collective-permute-start | bytes 1179656 | tf_op jit(solution)/shard_map/ppermute | solution.py:16
  435.1 5.3 collective-permute-done.4
  441.8 14.8 %psum.42 = f32[192]{0:T(256)S(1)} all-reduce(f32[192]{0:T(256)S(1)} %get-tuple-element.65), channel_id=1, replica_groups=mesh['gx'=4,'gy'=4,'gz'=2] {'gy','gz'}, use_global_device_ids=true, to_apply=%region_9.10 | all-reduce | flops 192 | bytes 1536 | tf_op jit(solution)/shard_map/psum | solution.py:176
  456.6 12.4 %psum.43 = f32[192]{0:T(256)} all-reduce(f32[192]{0:T(256)S(1)} %psum.42), channel_id=1, replica_groups=mesh['gx'=4,'gy'=4,'gz'=2] {'gx'}, use_global_device_ids=true, to_apply=%region_10.11 | all-reduce | flops 192 | bytes 1536 | tf_op jit(solution)/shard_map/psum | solution.py:175
  469.0 30.4 %all-reduce.5.cloned.1.call-done = (f32[192,576]{1,0:T(8,128)}, f32[192,192]{1,0:T(8,128)}) async-done(((f32[192,576]{1,0:T(8,128)}, f32[192,192]{1,0:T(8,128)}), (f32[192,576]{1,0:T(8,128)}, f32[192,192]{1,0:T(8,128)})) %all-reduce.5.cloned.1.call-update) | async-done | bytes 589840 | tf_op jit(solution)/shard_map/psum | solution.py:176
  506.0 36.2 %all-reduce.7.cloned.1.call-done = (f32[110592]{0:T(1024)}, f32[36864]{0:T(1024)}) async-done(((f32[110592]{0:T(1024)}, f32[36864]{0:T(1024)}), (f32[110592]{0:T(1024)}, f32[36864]{0:T(1024)})) %all-reduce.7.cloned.1.call-update) | async-done | bytes 589840 | tf_op jit(solution)/shard_map/psum | solution.py:175
  (284 shorter events, 256.1 us)
Async XLA Ops:
  7.2 9.3 %copy-start.7 = (bf16[16,16,3072]{2,1,0:T(8,128)(2,1)S(1)}, bf16[16,16,3072]{2,1,0:T(8,128)(2,1)}, u32[]{:S(2)}) copy-start(bf16[16,16,3072]{2,1,0:T(8,128)(2,1)} %param.8) | copy-start | bytes 4718596
  7.2 492.2 %all-reduce.5.cloned.1.call-start = ((), (), s32[]{:S(2)}) async-start(), calls=%async_computation | async-start | bytes 1376256 | tf_op jit(solution)/shard_map/psum | solution.py:176
  9.1 14.9 %collective-permute-start.2 = (bf16[4,16,3072]{2,1,0:T(8,128)(2,1)}, bf16[4,16,3072]{2,1,0:T(8,128)(2,1)}, u32[]{:S(2)}, u32[]{:S(2)}) collective-permute-start(bf16[4,16,3072]{2,1,0:T(8,128)(2,1)} %slice.74), channel_id=1, source_target_pairs={{8,0},{16,8},{24,16},{0,24},{9,1},{17,9},{25,17},{1,25},{10,2},{18... | collective-permute-start | bytes 1179656 | tf_op jit(solution)/shard_map/ppermute | solution.py:16
  15.9 15.3 %collective-permute-start = (bf16[4,16,3072]{2,1,0:T(8,128)(2,1)}, bf16[4,16,3072]{2,1,0:T(8,128)(2,1)}, u32[]{:S(2)}, u32[]{:S(2)}) collective-permute-start(bf16[4,16,3072]{2,1,0:T(8,128)(2,1)} %slice.68), channel_id=1, source_target_pairs={{8,0},{16,8},{24,16},{0,24},{9,1},{17,9},{25,17},{1,25},{10,2},{18... | collective-permute-start | bytes 1179656 | tf_op jit(solution)/shard_map/ppermute | solution.py:16
  25.4 10.4 %collective-permute-start.3 = (bf16[16,4,3072]{2,0,1:T(8,128)(2,1)S(1)}, bf16[16,4,3072]{2,0,1:T(8,128)(2,1)S(1)}, u32[]{:S(2)}, u32[]{:S(2)}) collective-permute-start(bf16[16,4,3072]{2,0,1:T(8,128)(2,1)S(1)} %pad_maximum_fusion.10), channel_id=1, source_target_pairs={{1,0},{2,1},{3,2},{4,3},{5,4},{6,5},{7,6},{0,7},{9,8},{10,9},{11,1... | collective-permute-start | bytes 1179656 | tf_op jit(solution)/shard_map/ppermute | solution.py:16
  33.4 10.8 %collective-permute-start.1 = (bf16[16,4,3072]{2,0,1:T(8,128)(2,1)}, bf16[16,4,3072]{2,0,1:T(8,128)(2,1)S(1)}, u32[]{:S(2)}, u32[]{:S(2)}) collective-permute-start(bf16[16,4,3072]{2,0,1:T(8,128)(2,1)} %pad_maximum_fusion.11), channel_id=1, source_target_pairs={{1,0},{2,1},{3,2},{4,3},{5,4},{6,5},{7,6},{0,7},{9,8},{10,9},{11,1... | collective-permute-start | bytes 1179656 | tf_op jit(solution)/shard_map/ppermute | solution.py:16
  91.9 4.4 copy-start.10
  97.7 5.6 %copy-start.12 = (bf16[6,32,512]{2,1,0:T(8,128)(2,1)S(1)}, bf16[6,32,512]{2,1,0:T(8,128)(2,1)}, u32[]{:S(2)}) copy-start(bf16[6,32,512]{2,1,0:T(8,128)(2,1)} %copy-done.11) | copy-start | bytes 589828 | tf_op jit(solution)/shard_map/while
  135.7 4.4 copy-start.10
  141.5 5.6 %copy-start.12 = (bf16[6,32,512]{2,1,0:T(8,128)(2,1)S(1)}, bf16[6,32,512]{2,1,0:T(8,128)(2,1)}, u32[]{:S(2)}) copy-start(bf16[6,32,512]{2,1,0:T(8,128)(2,1)} %copy-done.11) | copy-start | bytes 589828 | tf_op jit(solution)/shard_map/while
  180.6 4.4 copy-start.10
  186.3 5.6 %copy-start.12 = (bf16[6,32,512]{2,1,0:T(8,128)(2,1)S(1)}, bf16[6,32,512]{2,1,0:T(8,128)(2,1)}, u32[]{:S(2)}) copy-start(bf16[6,32,512]{2,1,0:T(8,128)(2,1)} %copy-done.11) | copy-start | bytes 589828 | tf_op jit(solution)/shard_map/while
  225.4 4.4 copy-start.10
  231.1 5.6 %copy-start.12 = (bf16[6,32,512]{2,1,0:T(8,128)(2,1)S(1)}, bf16[6,32,512]{2,1,0:T(8,128)(2,1)}, u32[]{:S(2)}) copy-start(bf16[6,32,512]{2,1,0:T(8,128)(2,1)} %copy-done.11) | copy-start | bytes 589828 | tf_op jit(solution)/shard_map/while
  270.2 4.4 copy-start.10
  276.0 5.6 %copy-start.12 = (bf16[6,32,512]{2,1,0:T(8,128)(2,1)S(1)}, bf16[6,32,512]{2,1,0:T(8,128)(2,1)}, u32[]{:S(2)}) copy-start(bf16[6,32,512]{2,1,0:T(8,128)(2,1)} %copy-done.11) | copy-start | bytes 589828 | tf_op jit(solution)/shard_map/while
  320.8 5.6 %copy-start.12 = (bf16[6,32,512]{2,1,0:T(8,128)(2,1)S(1)}, bf16[6,32,512]{2,1,0:T(8,128)(2,1)}, u32[]{:S(2)}) copy-start(bf16[6,32,512]{2,1,0:T(8,128)(2,1)} %copy-done.11) | copy-start | bytes 589828 | tf_op jit(solution)/shard_map/while
  365.7 5.6 %copy-start.12 = (bf16[6,32,512]{2,1,0:T(8,128)(2,1)S(1)}, bf16[6,32,512]{2,1,0:T(8,128)(2,1)}, u32[]{:S(2)}) copy-start(bf16[6,32,512]{2,1,0:T(8,128)(2,1)} %copy-done.11) | copy-start | bytes 589828 | tf_op jit(solution)/shard_map/while
  404.7 4.4 copy-start.10
  410.5 5.6 %copy-start.12 = (bf16[6,32,512]{2,1,0:T(8,128)(2,1)S(1)}, bf16[6,32,512]{2,1,0:T(8,128)(2,1)}, u32[]{:S(2)}) copy-start(bf16[6,32,512]{2,1,0:T(8,128)(2,1)} %copy-done.11) | copy-start | bytes 589828 | tf_op jit(solution)/shard_map/while
  428.2 12.2 %collective-permute-start.4 = (bf16[16,4,3072]{2,1,0:T(4,128)(2,1)S(1)}, bf16[16,4,3072]{2,1,0:T(4,128)(2,1)S(1)}, u32[]{:S(2)}, u32[]{:S(2)}) collective-permute-start(bf16[16,4,3072]{2,1,0:T(4,128)(2,1)S(1)} %slice.101), channel_id=1, source_target_pairs={{7,0},{0,1},{1,2},{2,3},{3,4},{4,5},{5,6},{6,7},{15,8},{8,9},{9,10... | collective-permute-start | bytes 1179656 | tf_op jit(solution)/shard_map/ppermute | solution.py:16
  440.4 62.8 %copy-start.2 = (bf16[16,16,3072]{2,1,0:T(8,128)(2,1)S(1)}, bf16[16,16,3072]{2,1,0:T(8,128)(2,1)}, u32[]{:S(2)}) copy-start(bf16[16,16,3072]{2,1,0:T(8,128)(2,1)} %param.9) | copy-start | bytes 4718596
  441.3 61.9 %collective-permute-start.5 = (bf16[4,16,3072]{2,1,0:T(8,128)(2,1)}, bf16[4,16,3072]{2,1,0:T(8,128)(2,1)}, u32[]{:S(2)}, u32[]{:S(2)}) collective-permute-start(bf16[4,16,3072]{2,1,0:T(8,128)(2,1)} %pad_maximum_fusion.9), channel_id=1, source_target_pairs={{24,0},{0,8},{8,16},{16,24},{25,1},{1,9},{9,17},{17,25},{26,2},{2,... | collective-permute-start | bytes 1179656 | tf_op jit(solution)/shard_map/ppermute | solution.py:16
  441.8 100.5 %all-reduce.7.cloned.1.call-start = ((), (), s32[]{:S(2)}) async-start(), calls=%async_computation.1 | async-start | bytes 1179648 | tf_op jit(solution)/shard_map/psum | solution.py:175
  (19 other events, 40.0 us)
Sparse Core Ops, SparseCore 0:
  441.9 57.4 all-reduce.4
  503.3 38.9 all-reduce.6
